TPU v7x, 128 devices: a whole 4x4x4 slice. The times are simulated.
128 devices in a mesh: blk: 16 (over y_hi, x, core), reg: 8 (over z, y_lo).
Axes of the slice: x: 4, y: 4 (y_hi: 2, y_lo: 2; y = y_hi * 2 + y_lo), z: 4, core: 2. Of those that a mesh axis runs over, the one named last changes fastest.
Arguments:
- inv_factor: bfloat16 [256, 1024, 1024], P(('blk', 'reg')), may hold values from -0.1875 to 0.1875
- border_global: bfloat16 [256, 1024, 512], P(('blk', 'reg')), may hold values from -6 to 6
- border_local: bfloat16 [256, 1024, 1536], P(('blk', 'reg')), may hold values from -6 to 6
- local_count: int32 [256], P(('blk', 'reg')), may hold values from 512 to 1536, as said below
Outputs:
- schur_global: float32 [512, 512], P('blk')
- schur_local: float32 [8, 1536, 1536], P('reg', 'blk')
- schur_cross: float32 [8, 512, 1536], P('reg', 'blk')
Inputs may be any that keep to these rules, and one draw needn't show every extreme that they name: Each block touches the first local_count of its region's local linking columns; some block touches exactly 1536 and some exactly 512.
All inputs are finite; a program needn't handle non-finite values.
Results may differ from a plain program's by a relative error of at most 0.0039.
Values may be sent and summed in bfloat16 or wider, within the bound.
No kernel may reach another device: no remote copies, remote signals or barrier semaphores. Data moves between devices by JAX's collectives and lax.ppermute only.
A program may use at most 128 MiB of HBM per device.

v0:
```python
import math
import jax
import jax.numpy as jnp
import numpy as np
from jax import lax
from jax.sharding import Mesh
from jax.sharding import PartitionSpec as P

BLK_AXES = ("yh", "x", "core")
REG_AXES = ("z", "yl")
CHIP_AXES = ("yh", "x")


def left_products(factor, border):
    return lax.dot_general(
        factor, border, (((1,), (1,)), ((0,), (0,))), preferred_element_type=jnp.float32
    ).astype(jnp.bfloat16)


def gram(first, second):
    return lax.dot_general(
        first, second, (((0,), (0,)), ((), ())), preferred_element_type=jnp.float32
    )


def owner_major(left, n_chip, n_core):
    rows, cols = left.shape
    per = cols // (n_chip * n_core)
    return left.reshape(rows, n_chip, n_core, per).transpose(0, 2, 1, 3).reshape(rows, cols)


def shards(inv_factor, border_global, border_local, local_count):
    blk_dev, order, _ = inv_factor.shape
    global_cols = border_global.shape[2]
    local_cols = border_local.shape[2]
    n_core = lax.axis_size("core")
    n_chip = lax.axis_size("yh") * lax.axis_size("x")
    n_blk = n_core * n_chip
    n_reg = lax.axis_size("z") * lax.axis_size("yl")
    columns = jnp.arange(local_cols, dtype=jnp.int32)
    masked = jnp.where(
        columns[None, None, :] < local_count[:, None, None],
        border_local,
        jnp.zeros((), border_local.dtype),
    )
    left_g = left_products(inv_factor, border_global).reshape(blk_dev * order, global_cols)
    left_l = left_products(inv_factor, masked).reshape(blk_dev * order, local_cols)
    part_top = gram(owner_major(left_g, n_chip, n_core), jnp.concatenate([left_g, left_l], axis=1))
    part_ll = gram(owner_major(left_l, n_chip, n_core), left_l)
    rows_g = global_cols // n_blk
    rows_l = local_cols // n_blk
    top = part_top.reshape(n_core, n_chip * rows_g, global_cols + local_cols)
    low = part_ll.reshape(n_core, n_chip * rows_l, local_cols)
    top = lax.psum_scatter(top, "core", scatter_dimension=0, tiled=True)
    low = lax.psum_scatter(low, "core", scatter_dimension=0, tiled=True)
    top = top.reshape(n_chip, rows_g * (global_cols + local_cols))
    low = low.reshape(n_chip, rows_l * local_cols)
    send = jnp.concatenate([top, low], axis=1).astype(jnp.bfloat16)
    got = lax.all_to_all(send, CHIP_AXES, 0, 0, tiled=True)
    summed = jnp.sum(got.astype(jnp.float32), axis=0)
    split = rows_g * (global_cols + local_cols)
    top = summed[:split].reshape(rows_g, global_cols + local_cols)
    low = summed[split:].reshape(rows_l, local_cols)
    all_blocks = blk_dev * n_blk * n_reg
    global_scale = 1.0 / math.sqrt(order * all_blocks)
    region_scale = 1.0 / math.sqrt(order * blk_dev * n_blk)
    global_part = lax.psum(top[:, :global_cols], REG_AXES)
    return (
        global_part * global_scale,
        (low * region_scale)[None],
        (top[:, global_cols:] * region_scale)[None],
    )


def solution(mesh):
    n_blk, n_reg = mesh.devices.shape
    devices = np.asarray(mesh.devices).reshape(2, n_blk // 4, 2, n_reg // 2, 2)
    fine = Mesh(devices, BLK_AXES + REG_AXES)
    every = BLK_AXES + REG_AXES
    placed = (P(every, None, None), P(every, None, None), P(every, None, None), P(every))
    return jax.shard_map(
        shards,
        mesh=fine,
        in_specs=placed,
        out_specs=(P(BLK_AXES, None), P(REG_AXES, BLK_AXES, None), P(REG_AXES, BLK_AXES, None)),
        check_vma=False,
    )
```

profile of v0, /device:TPU:0, one launch (start us, length us, event | category | flops | bytes accessed | tf_op | source)
XLA Modules:
  0.0 317.8 jit_solution(14593690149484430413)
XLA Ops:
  7.2 0.0 copy-start
  7.2 0.0 reduce-scatter.3.cloned.1.call-start
  7.2 0.9 iota_compare_fusion
  8.1 0.7 copy-done
  8.8 5.9 %convolution_convert_fusion = bf16[2,1024,512]{2,1,0:T(8,128)(2,1)} fusion(bf16[2,1024,1024]{2,1,0:T(8,128)(2,1)} %param.4, bf16[2,1024,512]{2,1,0:T(8,128)(2,1)S(1)} %copy-done), kind=kOutput, calls=%fused_computation.11 | convolution fusion | flops 2148532224 | bytes 8388608 | tf_op jit(solution)/shard_map/dot_general | solution.py:15
  14.7 6.3 %copy.16 = bf16[2,1024,512]{1,0,2:T(2,128)(2,1)} copy(bf16[2,1024,512]{2,1,0:T(8,128)(2,1)} %convolution_convert_fusion) | data formatting | bytes 4194304 | tf_op jit(solution)/shard_map/convert_element_type | solution.py:17
  21.0 3.3 %reshape_reshape.6 = bf16[2048,8,2,32]{0,3,2,1:T(8,128)(2,1)S(1)} reshape(bf16[2,1024,512]{1,0,2:T(2,128)(2,1)} %copy.16) | data formatting | bytes 4194304 | tf_op jit(solution)/shard_map/reshape;reshape | solution.py:29
  24.3 0.1 copy.17
  24.4 0.0 copy-start.3
  24.4 10.5 %fusion.6 = bf16[2,1536,1024]{1,2,0:T(8,128)(2,1)S(1)} fusion(bf16[2,1024,1024]{2,1,0:T(8,128)(2,1)} %param.4, bf16[2,1024,1536]{2,1,0:T(8,128)(2,1)} %param.6, pred[2,1536]{1,0:T(4,128)(4,1)S(1)} %iota_compare_fusion), kind=kOutput, calls=%fused_computation.9 | convolution fusion | flops 6448742400 | bytes 16780288 | tf_op jit(solution)/shard_map/dot_general | solution.py:15
  34.9 0.0 copy-start.2
  34.9 2.7 copy-done.2
  37.6 0.0 copy-done.3
  37.6 6.2 %fusion = f32[2,256,2048]{2,1,0:T(8,128)} fusion(bf16[2,256,2048]{2,1,0:T(8,128)(2,1)S(1)} %bitcast.40, bf16[2048,1536]{1,0:T(8,128)(2,1)S(1)} %bitcast.35, bf16[2048,512]{1,0:T(8,128)(2,1)S(1)} %bitcast.39), kind=kOutput, calls=%fused_computation.1 | convolution fusion | flops 4311744512 | bytes 14680064 | tf_op jit(solution)/shard_map/dot_general | solution.py:21
  43.8 0.0 reduce-scatter.3.cloned.1.call-update
  43.8 0.2 reduce-scatter.5.cloned.1.call-start
  44.1 16.7 %copy.19 = bf16[2,1024,1536]{1,0,2:T(2,128)(2,1)} copy(bf16[2,1024,1536]{2,1,0:T(8,128)(2,1)} %bitcast.36) | data formatting | bytes 12582912 | tf_op jit(solution)/shard_map/convert_element_type | solution.py:17
  60.8 11.1 %reshape_reshape.7 = bf16[2048,8,2,96]{0,3,2,1:T(8,128)(2,1)} reshape(bf16[2,1024,1536]{1,0,2:T(2,128)(2,1)} %copy.19) | data formatting | bytes 12582912 | tf_op jit(solution)/shard_map/reshape;reshape | solution.py:29
  71.9 3.4 %copy.20 = bf16[2048,2,8,96]{0,3,2,1:T(8,128)(2,1)S(1)} copy(bf16[2048,2,8,96]{0,3,1,2:T(8,128)(2,1)} %bitcast.33) | data formatting | bytes 12582912 | tf_op jit(solution)/shard_map/transpose | solution.py:29
  75.2 13.8 %fusion.13 = f32[2,768,1536]{2,1,0:T(8,128)} fusion(bf16[2,768,2048]{2,1,0:T(8,128)(2,1)S(1)} %bitcast.38, bf16[2048,1536,1]{1,0,2:T(8,128)(2,1)} %bitcast.37), kind=kOutput, calls=%fused_computation.19 | convolution fusion | flops 9663676416 | bytes 22020096 | tf_op jit(solution)/shard_map/dot_general | solution.py:21
  89.1 0.0 reduce-scatter.5.cloned.1.call-update
  89.1 0.0 all-reduce.2.cloned.1.call-start
  89.1 0.0 reduce-scatter.3.cloned.1.call-done
  89.2 1.7 convert.8
  90.9 1.7 concatenate.22
  92.6 19.1 %reduce-scatter.5.cloned.1.call-done = f32[1,768,1536]{2,1,0:T(8,128)} async-done(((f32[2,768,1536]{2,1,0:T(8,128)}), f32[1,768,1536]{2,1,0:T(8,128)}) %reduce-scatter.5.cloned.1.call-update) | async-done | bytes 4718608 | tf_op jit(solution)/shard_map/reduce_scatter | solution.py:55
  111.8 4.1 %convert.9 = bf16[1,768,1536]{2,1,0:T(8,128)(2,1)} convert(f32[1,768,1536]{2,1,0:T(8,128)} %reduce-scatter.5.cloned.1.call-done) | non-fusion elementwise | flops 1179648 | bytes 7077888 | tf_op jit(solution)/shard_map/convert.2
  115.9 6.6 %concatenate.23 = bf16[8,1,147456]{2,1,0:T(2,128)(2,1)} reshape(bf16[1,768,1536]{2,1,0:T(8,128)(2,1)} %convert.9) | data formatting | bytes 4718592 | tf_op jit(solution)/shard_map/concatenate | solution.py:58
  122.5 16.3 %pad_maximum_fusion = bf16[8,1,212992]{2,1,0:T(2,128)(2,1)} fusion(bf16[8,1,147456]{2,1,0:T(2,128)(2,1)} %concatenate.23, bf16[8,1,65536]{2,1,0:T(2,128)(2,1)S(1)} %concatenate.22), kind=kLoop, calls=%fused_computation.4 | loop fusion | flops 6815744 | bytes 6815744 | tf_op jit(solution)/shard_map/concatenate | solution.py:58
  138.8 0.5 broadcast.22
  139.3 23.5 %reduce.1 = bf16[8,212992]{1,0:T(8,128)(2,1)} reduce(bf16[8,1,212992]{2,1,0:T(2,128)(2,1)} %pad_maximum_fusion, bf16[]{:T(256)} %broadcast.22), dimensions={1}, to_apply=%pad_maximum_fusion.reduce_sub_computation | reduce | bytes 6815746 | tf_op jit(solution)/shard_map/concatenate | solution.py:58
  162.8 6.8 %reshape.109 = bf16[8,2,106496]{2,1,0:T(2,128)(2,1)} reshape(bf16[8,212992]{1,0:T(8,128)(2,1)} %reduce.1) | data formatting | bytes 6815744
  169.6 49.7 %all_to_all.6 = bf16[8,2,106496]{2,1,0:T(2,128)(2,1)} all-to-all(bf16[8,2,106496]{2,1,0:T(2,128)(2,1)} %reshape.109), channel_id=1, replica_groups=mesh['yh'=2,'x'=4,'core'=2,'z'=4,'yl'=2] {'yh','x'}, dimensions={0} | all-to-all | bytes 6815744 | tf_op jit(solution)/shard_map/all_to_all | solution.py:59
  219.3 0.0 copy-start.1
  219.3 8.2 %reshape.110 = bf16[8,1,212992]{2,1,0:T(2,128)(2,1)} reshape(bf16[8,2,106496]{2,1,0:T(2,128)(2,1)} %all_to_all.6) | data formatting | bytes 6815744
  227.6 10.0 %convert_reduce_fusion = f32[212992]{0:T(1024)S(1)} fusion(bf16[8,1,212992]{2,1,0:T(2,128)(2,1)} %reshape.110), kind=kLoop, calls=%fused_computation.5 | loop fusion | flops 3194880 | bytes 4259840 | tf_op jit(solution)/shard_map/reduce_sum | solution.py:60
  237.6 0.1 slice_multiply_fusion
  237.7 0.6 slice.28
  238.4 0.0 all-reduce.2.cloned.1.call-update
  238.4 0.7 fusion.10
  239.1 0.9 mul.32
  240.0 69.8 %all-reduce.2.cloned.1.call-done = f32[32,512]{1,0:T(8,128)} async-done(((f32[32,512]{1,0:T(8,128)}), f32[32,512]{1,0:T(8,128)}) %all-reduce.2.cloned.1.call-update) | async-done | bytes 65552 | tf_op jit(solution)/shard_map/psum | solution.py:67
  309.8 1.5 broadcast_multiply_fusion
  311.2 0.0 copy-done.1
  (2 shorter events, 0.1 us)
Async XLA Ops:
  7.2 1.6 copy-start
  7.2 82.0 %reduce-scatter.3.cloned.1.call-start = ((), (), s32[]{:S(2)}) async-start(), calls=%async_computation.3 | async-start | bytes 6291456 | tf_op jit(solution)/shard_map/reduce_scatter | solution.py:54
  24.4 13.2 %copy-start.3 = (bf16[2,1024,512]{2,1,0:T(8,128)(2,1)S(1)}, bf16[2,1024,512]{2,1,0:T(8,128)(2,1)}, u32[]{:S(2)}) copy-start(bf16[2,1024,512]{2,1,0:T(8,128)(2,1)} %convolution_convert_fusion) | copy-start | bytes 6291460
  34.9 2.7 copy-start.2
  43.8 67.9 %reduce-scatter.5.cloned.1.call-start = ((), (), s32[]{:S(2)}) async-start(), calls=%async_computation.4 | async-start | bytes 14155776 | tf_op jit(solution)/shard_map/reduce_scatter | solution.py:55
  89.1 220.7 %all-reduce.2.cloned.1.call-start = ((), (), s32[]{:S(2)}) async-start(), calls=%async_computation.5 | async-start | bytes 131072 | tf_op jit(solution)/shard_map/psum | solution.py:67
  219.3 91.9 %copy-start.1 = (bf16[2,1024,512]{2,1,0:T(8,128)(2,1)S(1)}, bf16[2,1024,512]{2,1,0:T(8,128)(2,1)}, u32[]{:S(2)}) copy-start(bf16[2,1024,512]{2,1,0:T(8,128)(2,1)} %param.5) | copy-start | bytes 6291460
Sparse Core Ops, SparseCore 0:
  44.0 17.2 reduce-scatter.2
  89.2 22.5 reduce-scatter.4
  238.5 71.2 all-reduce.1
where the time goes:
time: 319 us; the launch traced here: 318 us
  waiting for transfers between devices  89 us (28%)
  local copies, waits for them, and re-layouts  69.7 us (22%)
  other arithmetic  58.8 us (18%)
  blocking collectives  49.7 us (16%)
  matrix products  36.5 us (11%)
  between operations  13.9 us (4%)
    psum x1, waiting for transfers between devices, shards(): global_part = lax.psum(top[:, :global_cols], REG_AXES)  69.8 us
    all_to_all x1, blocking collectives, shards(): got = lax.all_to_all(send, CHIP_AXES, 0, 0, tiled=True)  49.7 us
    concatenate x2, other arithmetic, shards(): send = jnp.concatenate([top, low], axis=1).astype(jnp.bfloat16)  39.8 us
    convert_element_type x2, local copies, waits for them, and re-layouts, left_products(): return lax.dot_general(factor, border, (((1,), (1,)), ((0,), (0,))), pref...  23 us
    dot_general x2, matrix products, gram(): lax.dot_general(first, second, (((0,), (0,)), ((), ())), preferred_elemen...  20.1 us
    reduce_scatter x1, waiting for transfers between devices, shards(): low = lax.psum_scatter(low, 'core', scatter_dimension=0, tiled=True)  19.1 us
    unnamed x10, local copies, waits for them, and re-layouts  18.4 us
    dot_general x2, matrix products, left_products(): lax.dot_general(factor, border, (((1,), (1,)), ((0,), (0,))), preferred_e...  16.4 us
  transfers between devices with their start and end apart: 3, of which 2 were waited for; matrix products, arithmetic and copies ran while one was open for 16% of the time, Pallas kernels for 0%

commit v1 on v0

--- a/solution.py
+++ b/solution.py
@@ -64,7 +64,9 @@
     all_blocks = blk_dev * n_blk * n_reg
     global_scale = 1.0 / math.sqrt(order * all_blocks)
     region_scale = 1.0 / math.sqrt(order * blk_dev * n_blk)
-    global_part = lax.psum(top[:, :global_cols], REG_AXES)
+    block = top[:, :global_cols]
+    pieces = lax.all_gather(block, REG_AXES)
+    global_part = jnp.sum(pieces, axis=0)
     return (
         global_part * global_scale,
         (low * region_scale)[None],

time: 319 us -> 279 us (0.87)
  waiting for transfers between devices: 89 us -> 19.2 us
  blocking collectives: 49.7 us -> 80.1 us
    psum x1 -> x0, waiting for transfers between devices: 69.8 us -> none  [shards(): global_part = lax.psum(top[:, :global_cols], REG_AXES)]
    all_gather x0 -> x1, blocking collectives: none -> 30.4 us  [shards(): pieces = lax.all_gather(block, REG_AXES)]
  transfers between devices with their start and end apart: 3 -> 2, of which waited for: 2 -> 1; matrix products, arithmetic and copies ran while one was open for 16% -> 17% of each run, Pallas kernels for 0% -> 0%
where the time goes in v1:
time: 279 us; the launch traced here: 277 us
  blocking collectives  80.1 us (29%)
  local copies, waits for them, and re-layouts  69 us (25%)
  other arithmetic  58 us (21%)
  matrix products  36.5 us (13%)
  waiting for transfers between devices  19.2 us (7%)
  between operations  14.2 us (5%)
    all_to_all x1, blocking collectives, shards(): got = lax.all_to_all(send, CHIP_AXES, 0, 0, tiled=True)  49.7 us
    concatenate x2, other arithmetic, shards(): send = jnp.concatenate([top, low], axis=1).astype(jnp.bfloat16)  39.8 us
    all_gather x1, blocking collectives, shards(): pieces = lax.all_gather(block, REG_AXES)  30.4 us
    convert_element_type x2, local copies, waits for them, and re-layouts, left_products(): return lax.dot_general(factor, border, (((1,), (1,)), ((0,), (0,))), pref...  23 us
    dot_general x2, matrix products, gram(): lax.dot_general(first, second, (((0,), (0,)), ((), ())), preferred_elemen...  20.1 us
    reduce_scatter x1, waiting for transfers between devices, shards(): low = lax.psum_scatter(low, 'core', scatter_dimension=0, tiled=True)  19.2 us
    unnamed x10, local copies, waits for them, and re-layouts  18.4 us
    dot_general x2, matrix products, left_products(): lax.dot_general(factor, border, (((1,), (1,)), ((0,), (0,))), preferred_e...  16.4 us
  transfers between devices with their start and end apart: 2, of which 1 were waited for; matrix products, arithmetic and copies ran while one was open for 17% of the time, Pallas kernels for 0%

profile of v1, /device:TPU:0, one launch (start us, length us, event | category | flops | bytes accessed | tf_op | source)
XLA Modules:
  0.0 277.3 jit_solution(18078613678904243139)
XLA Ops:
  7.2 0.0 copy-start
  7.2 0.0 reduce-scatter.3.cloned.1.call-start
  7.2 0.9 iota_compare_fusion
  8.1 0.7 copy-done
  8.8 5.9 %convolution_convert_fusion = bf16[2,1024,512]{2,1,0:T(8,128)(2,1)} fusion(bf16[2,1024,1024]{2,1,0:T(8,128)(2,1)} %param.4, bf16[2,1024,512]{2,1,0:T(8,128)(2,1)S(1)} %copy-done), kind=kOutput, calls=%fused_computation.11 | convolution fusion | flops 2148532224 | bytes 8388608 | tf_op jit(solution)/shard_map/dot_general | solution.py:15
  14.7 6.3 %copy.16 = bf16[2,1024,512]{1,0,2:T(2,128)(2,1)} copy(bf16[2,1024,512]{2,1,0:T(8,128)(2,1)} %convolution_convert_fusion) | data formatting | bytes 4194304 | tf_op jit(solution)/shard_map/convert_element_type | solution.py:17
  21.0 3.3 %reshape_reshape.6 = bf16[2048,8,2,32]{0,3,2,1:T(8,128)(2,1)S(1)} reshape(bf16[2,1024,512]{1,0,2:T(2,128)(2,1)} %copy.16) | data formatting | bytes 4194304 | tf_op jit(solution)/shard_map/reshape;reshape | solution.py:29
  24.3 0.1 copy.17
  24.4 0.0 copy-start.3
  24.4 10.5 %fusion.6 = bf16[2,1536,1024]{1,2,0:T(8,128)(2,1)S(1)} fusion(bf16[2,1024,1024]{2,1,0:T(8,128)(2,1)} %param.4, bf16[2,1024,1536]{2,1,0:T(8,128)(2,1)} %param.6, pred[2,1536]{1,0:T(4,128)(4,1)S(1)} %iota_compare_fusion), kind=kOutput, calls=%fused_computation.9 | convolution fusion | flops 6448742400 | bytes 16780288 | tf_op jit(solution)/shard_map/dot_general | solution.py:15
  34.9 0.0 copy-start.2
  34.9 2.7 copy-done.2
  37.6 0.0 copy-done.3
  37.6 6.2 %fusion = f32[2,256,2048]{2,1,0:T(8,128)} fusion(bf16[2,256,2048]{2,1,0:T(8,128)(2,1)S(1)} %bitcast.41, bf16[2048,1536]{1,0:T(8,128)(2,1)S(1)} %bitcast.36, bf16[2048,512]{1,0:T(8,128)(2,1)S(1)} %bitcast.40), kind=kOutput, calls=%fused_computation.1 | convolution fusion | flops 4311744512 | bytes 14680064 | tf_op jit(solution)/shard_map/dot_general | solution.py:21
  43.8 0.0 reduce-scatter.3.cloned.1.call-update
  43.8 0.2 reduce-scatter.5.cloned.1.call-start
  44.1 16.7 %copy.19 = bf16[2,1024,1536]{1,0,2:T(2,128)(2,1)} copy(bf16[2,1024,1536]{2,1,0:T(8,128)(2,1)} %bitcast.37) | data formatting | bytes 12582912 | tf_op jit(solution)/shard_map/convert_element_type | solution.py:17
  60.8 11.1 %reshape_reshape.7 = bf16[2048,8,2,96]{0,3,2,1:T(8,128)(2,1)} reshape(bf16[2,1024,1536]{1,0,2:T(2,128)(2,1)} %copy.19) | data formatting | bytes 12582912 | tf_op jit(solution)/shard_map/reshape;reshape | solution.py:29
  71.9 3.4 %copy.20 = bf16[2048,2,8,96]{0,3,2,1:T(8,128)(2,1)S(1)} copy(bf16[2048,2,8,96]{0,3,1,2:T(8,128)(2,1)} %bitcast.34) | data formatting | bytes 12582912 | tf_op jit(solution)/shard_map/transpose | solution.py:29
  75.2 13.8 %fusion.13 = f32[2,768,1536]{2,1,0:T(8,128)} fusion(bf16[2,768,2048]{2,1,0:T(8,128)(2,1)S(1)} %bitcast.39, bf16[2048,1536,1]{1,0,2:T(8,128)(2,1)} %bitcast.38), kind=kOutput, calls=%fused_computation.19 | convolution fusion | flops 9663676416 | bytes 22020096 | tf_op jit(solution)/shard_map/dot_general | solution.py:21
  89.1 0.0 reduce-scatter.5.cloned.1.call-update
  89.1 0.0 reduce-scatter.3.cloned.1.call-done
  89.1 1.7 convert.8
  90.8 1.7 concatenate.22
  92.6 19.2 %reduce-scatter.5.cloned.1.call-done = f32[1,768,1536]{2,1,0:T(8,128)} async-done(((f32[2,768,1536]{2,1,0:T(8,128)}), f32[1,768,1536]{2,1,0:T(8,128)}) %reduce-scatter.5.cloned.1.call-update) | async-done | bytes 4718608 | tf_op jit(solution)/shard_map/reduce_scatter | solution.py:55
  111.8 4.1 %convert.9 = bf16[1,768,1536]{2,1,0:T(8,128)(2,1)} convert(f32[1,768,1536]{2,1,0:T(8,128)} %reduce-scatter.5.cloned.1.call-done) | non-fusion elementwise | flops 1179648 | bytes 7077888 | tf_op jit(solution)/shard_map/convert.2
  115.9 6.6 %concatenate.23 = bf16[8,1,147456]{2,1,0:T(2,128)(2,1)} reshape(bf16[1,768,1536]{2,1,0:T(8,128)(2,1)} %convert.9) | data formatting | bytes 4718592 | tf_op jit(solution)/shard_map/concatenate | solution.py:58
  122.5 16.3 %pad_maximum_fusion = bf16[8,1,212992]{2,1,0:T(2,128)(2,1)} fusion(bf16[8,1,147456]{2,1,0:T(2,128)(2,1)} %concatenate.23, bf16[8,1,65536]{2,1,0:T(2,128)(2,1)S(1)} %concatenate.22), kind=kLoop, calls=%fused_computation.4 | loop fusion | flops 6815744 | bytes 6815744 | tf_op jit(solution)/shard_map/concatenate | solution.py:58
  138.8 0.5 broadcast.22
  139.3 23.5 %reduce.1 = bf16[8,212992]{1,0:T(8,128)(2,1)} reduce(bf16[8,1,212992]{2,1,0:T(2,128)(2,1)} %pad_maximum_fusion, bf16[]{:T(256)} %broadcast.22), dimensions={1}, to_apply=%pad_maximum_fusion.reduce_sub_computation | reduce | bytes 6815746 | tf_op jit(solution)/shard_map/concatenate | solution.py:58
  162.8 6.8 %reshape.110 = bf16[8,2,106496]{2,1,0:T(2,128)(2,1)} reshape(bf16[8,212992]{1,0:T(8,128)(2,1)} %reduce.1) | data formatting | bytes 6815744
  169.6 49.7 %all_to_all.6 = bf16[8,2,106496]{2,1,0:T(2,128)(2,1)} all-to-all(bf16[8,2,106496]{2,1,0:T(2,128)(2,1)} %reshape.110), channel_id=1, replica_groups=mesh['yh'=2,'x'=4,'core'=2,'z'=4,'yl'=2] {'yh','x'}, dimensions={0} | all-to-all | bytes 6815744 | tf_op jit(solution)/shard_map/all_to_all | solution.py:59
  219.3 0.0 copy-start.1
  219.3 8.2 %reshape.111 = bf16[8,1,212992]{2,1,0:T(2,128)(2,1)} reshape(bf16[8,2,106496]{2,1,0:T(2,128)(2,1)} %all_to_all.6) | data formatting | bytes 6815744
  227.6 10.0 %convert_reduce_fusion = f32[212992]{0:T(1024)S(1)} fusion(bf16[8,1,212992]{2,1,0:T(2,128)(2,1)} %reshape.111), kind=kLoop, calls=%fused_computation.5 | loop fusion | flops 3194880 | bytes 4259840 | tf_op jit(solution)/shard_map/reduce_sum | solution.py:60
  237.7 0.7 fusion.10
  238.4 0.1 slice_multiply_fusion
  238.4 30.4 %all-gather = f32[256,512]{1,0:T(8,128)S(1)} all-gather(f32[32,512]{1,0:T(8,128)S(1)} %slice.28), channel_id=2, replica_groups=mesh['yh'=2,'x'=4,'core'=2,'z'=4,'yl'=2] {'z','yl'}, dimensions={0}, use_global_device_ids=true | all-gather | bytes 589824 | tf_op jit(solution)/shard_map/all_gather | solution.py:68
  268.9 0.6 broadcast_multiply_fusion
  269.5 0.9 mul.32
  270.4 0.0 copy-done.1
  (4 shorter events, 0.1 us)
Async XLA Ops:
  7.2 1.6 copy-start
  7.2 81.9 %reduce-scatter.3.cloned.1.call-start = ((), (), s32[]{:S(2)}) async-start(), calls=%async_computation.3 | async-start | bytes 6291456 | tf_op jit(solution)/shard_map/reduce_scatter | solution.py:54
  24.4 13.2 %copy-start.3 = (bf16[2,1024,512]{2,1,0:T(8,128)(2,1)S(1)}, bf16[2,1024,512]{2,1,0:T(8,128)(2,1)}, u32[]{:S(2)}) copy-start(bf16[2,1024,512]{2,1,0:T(8,128)(2,1)} %convolution_convert_fusion) | copy-start | bytes 6291460
  34.9 2.7 copy-start.2
  43.8 67.9 %reduce-scatter.5.cloned.1.call-start = ((), (), s32[]{:S(2)}) async-start(), calls=%async_computation.4 | async-start | bytes 14155776 | tf_op jit(solution)/shard_map/reduce_scatter | solution.py:55
  219.3 51.1 %copy-start.1 = (bf16[2,1024,512]{2,1,0:T(8,128)(2,1)S(1)}, bf16[2,1024,512]{2,1,0:T(8,128)(2,1)}, u32[]{:S(2)}) copy-start(bf16[2,1024,512]{2,1,0:T(8,128)(2,1)} %param.5) | copy-start | bytes 6291460
Sparse Core Ops, SparseCore 0:
  44.0 17.2 reduce-scatter.2
  89.2 22.5 reduce-scatter.4
